TPU v7x, 128 devices: a whole 4x4x4 slice. The times are simulated.
128 devices in a mesh: dom: 16 (over x, z_hi, core), cls: 8 (over z_lo, y).
Axes of the slice: x: 4, y: 4, z: 4 (z_hi: 2, z_lo: 2; z = z_hi * 2 + z_lo), core: 2. Of those that a mesh axis runs over, the one named last changes fastest.
Arguments:
- particles: bfloat16 [2048, 16384], P(('dom', 'cls')), may hold values from -6 to 6
- averages: float32 [256, 16384], P('cls'), may hold values from -4 to 4
- prior_mass: float32 [256], P('cls'), may hold values from 1 to 8
- group_ids: int32 [4, 2048, 1], P(None, ('dom', 'cls')), may hold values from 0 to 7; in each aligned block of 16 rows (0 to 15, 16 to 31, ..., all dimensions but the last counted through in order) at most 6 rows name the same one
- class_ids: int32 [4, 2048], P(None, ('dom', 'cls')), may hold values from 0 to 31
- rot_ids: int32 [4, 2048], P(None, ('dom', 'cls')), may hold values from 0 to 63
- weights: bfloat16 [4, 2048], P(None, ('dom', 'cls')), may hold values from 0.25 to 4
- owners: int32 [4], replicated, may hold values from 0 to 7
Outputs:
- scores: float32 [4, 2048, 2048], P(None, ('dom', 'cls'))
- final_averages: float32 [256, 16384], P('cls')
Inputs may be any that keep to these rules, and one draw needn't show every extreme that they name: `group_ids`: in every step, at most 6 of the 16 particles of one device name one class group; in every step some device's particles reach 6 for some group.
All inputs are finite; a program needn't handle non-finite values.
Results may differ from a plain program's by a relative error of at most 0.0027.
Values may be sent and summed in bfloat16 or wider, within the bound.
No kernel may reach another device: no remote copies, remote signals or barrier semaphores. Data moves between devices by JAX's collectives and lax.ppermute only.
A program may use at most 256 MiB of HBM per device.

v0:
```python
import math
import jax
import jax.numpy as jnp
from jax import lax
from jax.sharding import PartitionSpec as P

RADII = 128
ANGLES = 128
ROT = 64
STEPS = 4
ASTEP = 2


def rotate_each(cube, shifts):
    src = jnp.arange(ANGLES, dtype=jnp.int32)
    dst = (src[None, :, None] + shifts[:, None, None]) % ANGLES
    perm = (dst == src[None, None, :]).astype(cube.dtype)
    out = jnp.einsum("iab,ibc->iac", cube, perm, preferred_element_type=jnp.float32)
    return out.astype(cube.dtype)


def per_device(particles, averages, prior_mass, group_ids, class_ids, rot_ids, weights, owners):
    per_dev = particles.shape[0]
    pixels = particles.shape[1]
    groups = lax.axis_size("cls")
    doms = lax.axis_size("dom")
    chunk = pixels // doms
    per_group = averages.shape[0]
    capacity = per_dev * 3 // 8
    slots = groups * capacity
    me_dom = lax.axis_index("dom")
    me_cls = lax.axis_index("cls")
    cube = particles.reshape(per_dev, RADII, ANGLES)
    doubled = jnp.concatenate([cube, cube], axis=2)
    scale = 1.0 / math.sqrt(pixels)
    turns_block = min(ROT, max(8, 512 // per_dev))
    block_starts = list(range(0, ROT, turns_block))
    send_img = []
    send_wts = []
    for step in range(STEPS):
        shifts = rot_ids[step] * ASTEP
        rotated = rotate_each(cube, shifts).reshape(per_dev, pixels)
        target = group_ids[step, :, 0]
        onehot_group = (target[:, None] == jnp.arange(groups, dtype=jnp.int32)[None, :]).astype(
            jnp.int32
        )
        rank = jnp.sum((jnp.cumsum(onehot_group, axis=0) - 1) * onehot_group, axis=1)
        slot_of = target * capacity + rank
        placing = (slot_of[None, :] == jnp.arange(slots, dtype=jnp.int32)[:, None]).astype(
            jnp.bfloat16
        )
        images = jnp.dot(placing, rotated, preferred_element_type=jnp.float32).astype(jnp.bfloat16)
        images = images.reshape(groups, capacity, doms, chunk).transpose(2, 0, 1, 3)
        send_img.append(images)
        class_hot = (
            class_ids[step][:, None] == jnp.arange(per_group, dtype=jnp.int32)[None, :]
        ).astype(jnp.bfloat16)
        weighted_hot = class_hot * weights[step][:, None]
        wts = jnp.dot(placing, weighted_hot, preferred_element_type=jnp.float32).astype(
            jnp.bfloat16
        )
        wts = jnp.broadcast_to(
            wts.reshape(1, groups, capacity, per_group), (doms, groups, capacity, per_group)
        )
        send_wts.append(wts)
    send_img = jnp.stack(send_img, axis=2).reshape(doms * groups, STEPS, capacity, chunk)
    send_wts = jnp.stack(send_wts, axis=2).reshape(doms * groups, STEPS, capacity, per_group)
    got_img = lax.all_to_all(send_img, ("dom", "cls"), 0, 0, tiled=True)
    got_wts = lax.all_to_all(send_wts, ("dom", "cls"), 0, 0, tiled=True)
    totals = lax.dot_general(
        got_wts, got_img, (((0, 2), (0, 2)), ((1,), (1,))), preferred_element_type=jnp.float32
    )
    mass = jnp.sum(got_wts.astype(jnp.float32), axis=(0, 2))
    current = lax.dynamic_slice_in_dim(averages, me_dom * chunk, chunk, axis=1)
    ref_chunks = []
    for step in range(STEPS):
        current = (prior_mass[:, None] * current + totals[step]) / (prior_mass + mass[step])[
            :, None
        ]
        piece = current.astype(jnp.bfloat16)
        piece = jnp.where(me_cls == owners[step], piece, jnp.zeros_like(piece))
        ref_chunks.append(piece)
    ref_chunks = lax.psum(jnp.stack(ref_chunks, axis=0), "cls")
    all_refs = lax.all_gather(ref_chunks, "dom", axis=0, tiled=False)
    all_refs = all_refs.transpose(1, 2, 0, 3).reshape(STEPS, per_group, pixels)
    final = lax.all_gather(current, "dom", axis=0, tiled=False)
    final = final.transpose(1, 0, 2).reshape(per_group, pixels)
    all_scores = []
    for step in range(STEPS):
        refs = all_refs[step]
        pieces = []
        for first in block_starts:
            count = min(turns_block, ROT - first)
            views = [
                doubled[:, :, ANGLES - turn * ASTEP : 2 * ANGLES - turn * ASTEP]
                for turn in range(first, first + count)
            ]
            rolled = jnp.stack(views, axis=1).reshape(per_dev * count, pixels)
            product = lax.dot_general(
                rolled, refs, (((1,), (1,)), ((), ())), preferred_element_type=jnp.float32
            )
            pieces.append(product.reshape(per_dev, count * per_group))
        stacked = jnp.concatenate(pieces, axis=1)
        all_scores.append(stacked * scale)
    return (jnp.stack(all_scores, axis=0), final)


def solution(mesh):
    return jax.shard_map(
        per_device,
        mesh=mesh,
        in_specs=(
            P(("dom", "cls"), None),
            P("cls", None),
            P("cls"),
            P(None, ("dom", "cls"), None),
            P(None, ("dom", "cls")),
            P(None, ("dom", "cls")),
            P(None, ("dom", "cls")),
            P(),
        ),
        out_specs=(P(None, ("dom", "cls"), None), P("cls", None)),
        check_vma=False,
    )
```

profile of v0, /device:TPU:1, one launch (start us, length us, event | category | flops | bytes accessed | tf_op | source)
XLA Modules:
  0.0 466.9 jit_solution(8276902115353094044)
XLA Ops:
  14.4 1.3 reshape.477
  15.7 11.7 %all-to-all-start = ((bf16[128,2,384]{2,1,0:T(2,128)(2,1)}), bf16[128,2,384]{2,1,0:T(2,128)(2,1)S(1)}, u32[]{:S(2)}, u32[]{:S(2)}) async-start(bf16[128,2,384]{2,1,0:T(2,128)(2,1)} %reshape.477), calls=%async_computation | async-start | bytes 393216 | tf_op jit(solution)/shard_map/all_to_all | solution.py:69
  28.2 1.1 copy.284
  41.1 1.3 copy.363
  42.4 3.2 pad_maximum_fusion
  45.6 10.3 %copy.227 = bf16[128,4,6,1024]{3,1,2,0:T(4,128)(2,1)} copy(bf16[128,4,6,1024]{3,0,2,1:T(8,128)(2,1)} %pad_maximum_fusion) | data formatting | bytes 12582912 | tf_op jit(solution)/shard_map/stack | solution.py:66
  55.9 10.2 %all-to-all-start.1 = ((bf16[128,4,6,1024]{3,1,2,0:T(4,128)(2,1)}), bf16[128,4,6,1024]{3,1,2,0:T(4,128)(2,1)}, u32[]{:S(2)}, u32[]{:S(2)}) async-start(bf16[128,4,6,1024]{3,1,2,0:T(4,128)(2,1)} %copy.227), calls=%async_computation.1 | async-start | bytes 12582912 | tf_op jit(solution)/shard_map/all_to_all | solution.py:68
  71.4 1.1 fusion.104
  72.5 1.1 fusion.103
  74.6 1.0 fusion.101
  76.6 1.0 fusion.99
  78.7 1.0 fusion.97
  79.7 1.1 fusion.96
  82.8 1.1 fusion.93
  85.1 60.6 %all-to-all-done.1 = bf16[128,4,6,1024]{3,1,2,0:T(4,128)(2,1)} async-done(((bf16[128,4,6,1024]{3,1,2,0:T(4,128)(2,1)}), bf16[128,4,6,1024]{3,1,2,0:T(4,128)(2,1)}, u32[]{:S(2)}, u32[]{:S(2)}) %all-to-all-start.1) | async-done | bytes 6291488 | tf_op jit(solution)/shard_map/all_to_all | solution.py:68
  145.6 9.7 %fusion.30 = f32[4,32,1024]{2,1,0:T(8,128)S(1)} fusion(bf16[128,4,6,1024]{3,1,2,0:T(4,128)(2,1)} %all-to-all-done.1, bf16[128,4,6,32]{3,1,2,0:T(4,128)(2,1)S(1)} %bitcast.549), kind=kOutput, calls=%fused_computation.44 | convolution fusion | flops 201326592 | bytes 7012352 | tf_op jit(solution)/shard_map/dot_general | solution.py:70
  160.3 1.0 fusion.90
  161.4 1.0 fusion.89
  162.4 1.0 fusion.88
  163.4 1.0 fusion.87
  164.5 1.0 fusion.86
  165.5 1.0 fusion.85
  167.6 1.0 fusion.83
  170.6 1.0 fusion.80
  171.7 1.1 fusion.79
  173.7 1.0 fusion.77
  174.8 1.0 fusion.76
  175.8 1.1 fusion.75
  176.9 51.4 %all-reduce.2.cloned.1.call-done = bf16[1,4,32,1024]{3,2,1,0:T(8,128)(2,1)} async-done(((bf16[1,4,32,1024]{3,2,1,0:T(8,128)(2,1)}), bf16[1,4,32,1024]{3,2,1,0:T(8,128)(2,1)}) %all-reduce.2.cloned.1.call-update) | async-done | bytes 262160 | tf_op jit(solution)/shard_map/psum | solution.py:83
  229.3 14.2 %copy.209 = bf16[16,32,128,128]{3,2,1,0:T(8,128)(2,1)} copy(bf16[16,32,128,128]{3,2,0,1:T(8,128)(2,1)} %fusion.74) | data formatting | bytes 33554432 | tf_op jit(solution)/shard_map/stack | solution.py:98
  243.4 1.0 fusion.72
  245.5 1.0 fusion.70
  246.5 1.0 fusion.69
  247.6 1.0 fusion.68
  248.6 1.0 fusion.67
  249.6 1.0 fusion.66
  250.7 1.0 fusion.65
  253.8 1.0 fusion.62
  258.8 1.0 fusion.57
  260.9 1.0 fusion.55
  261.9 1.0 fusion.54
  263.0 1.0 fusion.53
  268.1 1.0 fusion.48
  273.2 1.0 fusion.43
  274.2 1.0 fusion.42
  275.3 3.2 copy.283
  278.4 10.8 %all-gather.4.cloned.1.call-done = bf16[16,4,32,1024]{3,2,1,0:T(8,128)(2,1)} async-done(((bf16[1,4,32,1024]{3,2,1,0:T(8,128)(2,1)}), bf16[16,4,32,1024]{3,2,1,0:T(8,128)(2,1)}) %all-gather.4.cloned.1.call-update) | async-done | bytes 4194320 | tf_op jit(solution)/shard_map/all_gather | solution.py:84
  289.2 2.6 fusion.172
  292.0 1.2 copy.298
  293.3 18.1 %fusion = f32[512,32]{1,0:T(8,128)} fusion(bf16[32,16384]{1,0:T(8,128)(2,1)S(1)} %bitcast.574, bf16[64,8,128,128]{3,2,1,0:T(8,128)(2,1)} %bitcast.216), kind=kOutput, calls=%fused_computation.4 | convolution fusion | flops 536870912 | bytes 17891328 | tf_op jit(solution)/shard_map/dot_general | solution.py:99
  311.4 24.1 %fusion.2 = f32[512,32]{1,0:T(8,128)} fusion(bf16[32,16384]{1,0:T(8,128)(2,1)} %bitcast.576, bf16[64,8,128,128]{3,2,1,0:T(8,128)(2,1)} %bitcast.216), kind=kOutput, calls=%fused_computation.6 | convolution fusion | flops 536870912 | bytes 17891328 | tf_op jit(solution)/shard_map/dot_general | solution.py:99
  335.5 18.4 %fusion.8 = f32[512,32]{1,0:T(8,128)S(1)} fusion(bf16[32,16384]{1,0:T(8,128)(2,1)} %bitcast.575, bf16[64,8,128,128]{3,2,1,0:T(8,128)(2,1)S(1)} %bitcast.545), kind=kOutput, calls=%fused_computation.12 | convolution fusion | flops 536870912 | bytes 17891328 | tf_op jit(solution)/shard_map/dot_general | solution.py:99
  353.9 18.8 %fusion.10 = f32[512,32]{1,0:T(8,128)S(1)} fusion(bf16[32,16384]{1,0:T(8,128)(2,1)} %bitcast.577, bf16[64,8,128,128]{3,2,1,0:T(8,128)(2,1)S(1)} %bitcast.546), kind=kOutput, calls=%fused_computation.14 | convolution fusion | flops 536870912 | bytes 17891328 | tf_op jit(solution)/shard_map/dot_general | solution.py:99
  372.7 1.1 copy.297
  373.7 23.9 %fusion.4 = f32[512,32]{1,0:T(8,128)} fusion(bf16[32,16384]{1,0:T(8,128)(2,1)} %bitcast.580, bf16[64,8,128,128]{3,2,1,0:T(8,128)(2,1)} %bitcast.216), kind=kOutput, calls=%fused_computation.8 | convolution fusion | flops 536870912 | bytes 17891328 | tf_op jit(solution)/shard_map/dot_general | solution.py:99
  397.7 18.2 %fusion.12 = f32[512,32]{1,0:T(8,128)} fusion(bf16[32,16384]{1,0:T(8,128)(2,1)S(1)} %bitcast.581, bf16[64,8,128,128]{3,2,1,0:T(8,128)(2,1)S(1)} %bitcast.547), kind=kOutput, calls=%fused_computation.16 | convolution fusion | flops 536870912 | bytes 17891328 | tf_op jit(solution)/shard_map/dot_general | solution.py:99
  416.0 17.6 %fusion.6 = f32[512,32]{1,0:T(8,128)} fusion(bf16[32,16384]{1,0:T(8,128)(2,1)S(1)} %bitcast.578, bf16[64,8,128,128]{3,2,1,0:T(8,128)(2,1)} %bitcast.216), kind=kOutput, calls=%fused_computation.10 | convolution fusion | flops 536870912 | bytes 17891328 | tf_op jit(solution)/shard_map/dot_general | solution.py:99
  433.6 17.9 %fusion.14 = f32[512,32]{1,0:T(8,128)} fusion(bf16[32,16384]{1,0:T(8,128)(2,1)S(1)} %bitcast.579, bf16[64,8,128,128]{3,2,1,0:T(8,128)(2,1)S(1)} %bitcast.548), kind=kOutput, calls=%fused_computation.18 | convolution fusion | flops 536870912 | bytes 17891328 | tf_op jit(solution)/shard_map/dot_general | solution.py:99
  451.5 1.1 concatenate.71
  452.6 1.1 concatenate.68
  453.7 1.1 concatenate.62
  454.7 1.1 concatenate.65
  455.8 1.1 concatenate.61
  456.9 1.1 concatenate.64
  (132 shorter events, 55.6 us)
Async XLA Ops:
  15.7 40.2 %all-to-all-start = ((bf16[128,2,384]{2,1,0:T(2,128)(2,1)}), bf16[128,2,384]{2,1,0:T(2,128)(2,1)S(1)}, u32[]{:S(2)}, u32[]{:S(2)}) async-start(bf16[128,2,384]{2,1,0:T(2,128)(2,1)} %reshape.477), calls=%async_computation | async-start | bytes 393216 | tf_op jit(solution)/shard_map/all_to_all | solution.py:69
  42.4 23.7 %copy-start.2 = (s32[4]{0:T(128)S(1)}, s32[4]{0:T(128)}, u32[]{:S(2)}) copy-start(s32[4]{0:T(128)} %param.15) | copy-start | bytes 52
  55.9 29.2 %copy-start.3 = (f32[32]{0:T(128)S(1)}, f32[32]{0:T(128)}, u32[]{:S(2)}) copy-start(f32[32]{0:T(128)} %param.10) | copy-start | bytes 388
  55.9 89.7 %all-to-all-start.1 = ((bf16[128,4,6,1024]{3,1,2,0:T(4,128)(2,1)}), bf16[128,4,6,1024]{3,1,2,0:T(4,128)(2,1)}, u32[]{:S(2)}, u32[]{:S(2)}) async-start(bf16[128,4,6,1024]{3,1,2,0:T(4,128)(2,1)} %copy.227), calls=%async_computation.1 | async-start | bytes 12582912 | tf_op jit(solution)/shard_map/all_to_all | solution.py:68
  66.1 162.2 %all-reduce.2.cloned.1.call-start = ((), (), s32[]{:S(2)}) async-start(), calls=%async_computation.2 | async-start | bytes 524288 | tf_op jit(solution)/shard_map/psum | solution.py:83
  158.0 117.3 %all-gather.6.cloned.1.call-start = ((), (), s32[]{:S(2)}) async-start(), calls=%async_computation.4 | async-start | bytes 2228224 | tf_op jit(solution)/shard_map/all_gather | solution.py:86
  160.3 129.0 %all-gather.4.cloned.1.call-start = ((), (), s32[]{:S(2)}) async-start(), calls=%async_computation.3 | async-start | bytes 4456448 | tf_op jit(solution)/shard_map/all_gather | solution.py:84
  292.0 1.3 copy-start
  293.3 42.2 %slice-start = ((s8[16777216]{0:T(1024)(128)(4,1)}), s8[4194304]{0:T(1024)(128)(4,1)S(1)}, s32[]{:S(2)}) async-start(s8[16777216]{0:T(1024)(128)(4,1)} %bitcast.543), calls=%async_computation.5 | async-start | bytes 8388608
  293.3 42.2 %slice-start.1 = ((s8[16777216]{0:T(1024)(128)(4,1)}), s8[4194304]{0:T(1024)(128)(4,1)S(1)}, s32[]{:S(2)}) async-start(s8[16777216]{0:T(1024)(128)(4,1)} %bitcast.543), calls=%async_computation.6 | async-start | bytes 8388608
  311.4 24.1 %slice-start.2 = ((s8[16777216]{0:T(1024)(128)(4,1)}), s8[4194304]{0:T(1024)(128)(4,1)S(1)}, s32[]{:S(2)}) async-start(s8[16777216]{0:T(1024)(128)(4,1)} %bitcast.543), calls=%async_computation.7 | async-start | bytes 8388608
  311.4 24.1 %slice-start.3 = ((s8[16777216]{0:T(1024)(128)(4,1)}), s8[4194304]{0:T(1024)(128)(4,1)S(1)}, s32[]{:S(2)}) async-start(s8[16777216]{0:T(1024)(128)(4,1)} %bitcast.543), calls=%async_computation.8 | async-start | bytes 8388608
  373.7 23.9 %copy-start.1 = (bf16[4,8,16,1024]{3,1,2,0:T(8,128)(2,1)S(1)}, bf16[4,8,16,1024]{3,1,2,0:T(8,128)(2,1)}, u32[]{:S(2)}) copy-start(bf16[4,8,16,1024]{3,1,2,0:T(8,128)(2,1)} %copy.297) | copy-start | bytes 3145732
Sparse Core Ops, SparseCore 0:
  158.1 70.0 all-reduce.1
Sparse Core Ops, SparseCore 1:
  161.4 49.9 all-gather.5
  228.3 60.8 all-gather.3
where the time goes:
time: 471 us; the launch traced here: 467 us
  matrix products  172 us (37%)
  waiting for transfers between devices  123 us (26%)
  local copies, waits for them, and re-layouts  121 us (26%)
  starting transfers between devices  22.1 us (5%)
  between operations  18.8 us (4%)
  other arithmetic  10.2 us (2%)
    dot_general x8, matrix products, per_device(): lax.dot_general(rolled, refs, (((1,), (1,)), ((), ())), preferred_element...  157 us
    unnamed x90, local copies, waits for them, and re-layouts  72.6 us
    all_to_all x1, waiting for transfers between devices, per_device(): got_img = lax.all_to_all(send_img, ('dom', 'cls'), 0, 0, tiled=True)  60.6 us
    psum x1, waiting for transfers between devices, per_device(): ref_chunks = lax.psum(jnp.stack(ref_chunks, axis=0), 'cls')  51.4 us
    another operation x3, local copies, waits for them, and re-layouts, per_device(): rolled = jnp.stack(views, axis=1).reshape(per_dev * count, pixels)  16.2 us
    all_to_all x1, starting transfers between devices, per_device(): got_wts = lax.all_to_all(send_wts, ('dom', 'cls'), 0, 0, tiled=True)  11.7 us
    all_gather x1, waiting for transfers between devices, per_device(): all_refs = lax.all_gather(ref_chunks, 'dom', axis=0, tiled=False)  10.8 us
    another operation x1, local copies, waits for them, and re-layouts, per_device(): jnp.stack(send_img, axis=2).reshape(doms * groups, STEPS, capacity, chunk)  10.3 us
  transfers between devices with their start and end apart: 5, of which 3 were waited for; matrix products, arithmetic and copies ran while one was open for 24% of the time, Pallas kernels for 0%

commit v1 on v0

--- a/solution.py
+++ b/solution.py
@@ -80,7 +80,7 @@
         piece = current.astype(jnp.bfloat16)
         piece = jnp.where(me_cls == owners[step], piece, jnp.zeros_like(piece))
         ref_chunks.append(piece)
-    ref_chunks = lax.psum(jnp.stack(ref_chunks, axis=0), "cls")
+    ref_chunks = jnp.sum(lax.all_gather(jnp.stack(ref_chunks, axis=0), "cls"), axis=0)
     all_refs = lax.all_gather(ref_chunks, "dom", axis=0, tiled=False)
     all_refs = all_refs.transpose(1, 2, 0, 3).reshape(STEPS, per_group, pixels)
     final = lax.all_gather(current, "dom", axis=0, tiled=False)

time: 471 us -> 489 us (1.038)
  waiting for transfers between devices: 123 us -> 140 us
    psum x1 -> x0, waiting for transfers between devices: 51.4 us -> none  [per_device(): ref_chunks = lax.psum(jnp.stack(ref_chunks, axis=0), 'cls')]
    all_gather x1, waiting for transfers between devices: 10.8 us -> 54.6 us  [per_device(): all_refs = lax.all_gather(ref_chunks, 'dom', axis=0, tiled=False)]
    all_to_all x1, waiting for transfers between devices: 60.6 us -> 75 us  [per_device(): got_img = lax.all_to_all(send_img, ('dom', 'cls'), 0, 0, tiled=True)]
    all_gather x1, waiting for transfers between devices: 0.01 us -> 5.96 us  [per_device(): final = lax.all_gather(current, 'dom', axis=0, tiled=False)]
  transfers between devices with their start and end apart: 5 -> 5, of which waited for: 3 -> 4; matrix products, arithmetic and copies ran while one was open for 24% -> 24% of each run, Pallas kernels for 0% -> 0%
where the time goes in v1:
time: 489 us; the launch traced here: 485 us
  matrix products  172 us (35%)
  waiting for transfers between devices  140 us (29%)
  local copies, waits for them, and re-layouts  121 us (25%)
  starting transfers between devices  22.4 us (5%)
  between operations  17 us (3%)
  other arithmetic  13 us (3%)
    dot_general x8, matrix products, per_device(): lax.dot_general(rolled, refs, (((1,), (1,)), ((), ())), preferred_element...  157 us
    all_to_all x1, waiting for transfers between devices, per_device(): got_img = lax.all_to_all(send_img, ('dom', 'cls'), 0, 0, tiled=True)  75 us
    unnamed x90, local copies, waits for them, and re-layouts  72.6 us
    all_gather x1, waiting for transfers between devices, per_device(): all_refs = lax.all_gather(ref_chunks, 'dom', axis=0, tiled=False)  54.6 us
    another operation x3, local copies, waits for them, and re-layouts, per_device(): rolled = jnp.stack(views, axis=1).reshape(per_dev * count, pixels)  16.4 us
    all_to_all x1, starting transfers between devices, per_device(): got_wts = lax.all_to_all(send_wts, ('dom', 'cls'), 0, 0, tiled=True)  11.7 us
    another operation x1, local copies, waits for them, and re-layouts, per_device(): jnp.stack(send_img, axis=2).reshape(doms * groups, STEPS, capacity, chunk)  10.3 us
    all_to_all x1, starting transfers between devices, per_device(): got_img = lax.all_to_all(send_img, ('dom', 'cls'), 0, 0, tiled=True)  10.2 us
  transfers between devices with their start and end apart: 5, of which 4 were waited for; matrix products, arithmetic and copies ran while one was open for 24% of the time, Pallas kernels for 0%

profile of v1, /device:TPU:1, one launch (start us, length us, event | category | flops | bytes accessed | tf_op | source)
XLA Modules:
  0.0 485.2 jit_solution(6489368773196271245)
XLA Ops:
  13.6 1.3 reshape.479
  14.9 11.7 %all-to-all-start = ((bf16[128,2,384]{2,1,0:T(2,128)(2,1)}), bf16[128,2,384]{2,1,0:T(2,128)(2,1)S(1)}, u32[]{:S(2)}, u32[]{:S(2)}) async-start(bf16[128,2,384]{2,1,0:T(2,128)(2,1)} %reshape.479), calls=%async_computation | async-start | bytes 393216 | tf_op jit(solution)/shard_map/all_to_all | solution.py:69
  27.4 1.1 copy.342
  40.3 1.1 copy.421
  41.4 3.3 pad_maximum_fusion
  44.6 10.3 %copy.285 = bf16[128,4,6,1024]{3,1,2,0:T(4,128)(2,1)} copy(bf16[128,4,6,1024]{3,0,2,1:T(8,128)(2,1)} %pad_maximum_fusion) | data formatting | bytes 12582912 | tf_op jit(solution)/shard_map/stack | solution.py:66
  54.9 10.2 %all-to-all-start.1 = ((bf16[128,4,6,1024]{3,1,2,0:T(4,128)(2,1)}), bf16[128,4,6,1024]{3,1,2,0:T(4,128)(2,1)}, u32[]{:S(2)}, u32[]{:S(2)}) async-start(bf16[128,4,6,1024]{3,1,2,0:T(4,128)(2,1)} %copy.285), calls=%async_computation.1 | async-start | bytes 12582912 | tf_op jit(solution)/shard_map/all_to_all | solution.py:68
  69.7 75.0 %all-to-all-done.1 = bf16[128,4,6,1024]{3,1,2,0:T(4,128)(2,1)} async-done(((bf16[128,4,6,1024]{3,1,2,0:T(4,128)(2,1)}), bf16[128,4,6,1024]{3,1,2,0:T(4,128)(2,1)}, u32[]{:S(2)}, u32[]{:S(2)}) %all-to-all-start.1) | async-done | bytes 6291488 | tf_op jit(solution)/shard_map/all_to_all | solution.py:68
  144.7 9.7 %fusion.30 = f32[4,32,1024]{2,1,0:T(8,128)S(1)} fusion(bf16[128,4,6,1024]{3,1,2,0:T(4,128)(2,1)} %all-to-all-done.1, bf16[128,4,6,32]{3,1,2,0:T(4,128)(2,1)S(1)} %bitcast.550), kind=kOutput, calls=%fused_computation.44 | convolution fusion | flops 201326592 | bytes 7012352 | tf_op jit(solution)/shard_map/dot_general | solution.py:70
  159.3 1.1 fusion.104
  160.4 1.1 fusion.103
  164.5 1.0 fusion.99
  166.6 1.0 fusion.97
  167.6 1.1 fusion.96
  170.7 1.1 fusion.93
  173.9 1.0 fusion.90
  174.9 1.0 fusion.89
  176.0 1.0 fusion.88
  177.0 1.0 fusion.87
  178.0 1.0 fusion.86
  179.1 1.0 fusion.85
  184.2 1.0 fusion.80
  185.2 1.1 fusion.79
  187.3 1.0 fusion.77
  188.3 1.0 fusion.76
  189.4 1.1 fusion.75
  190.4 4.4 all-gather.7.cloned.1.call-done
  194.8 2.7 reduce_sum.62
  198.6 14.3 %copy.267 = bf16[16,32,128,128]{3,2,1,0:T(8,128)(2,1)} copy(bf16[16,32,128,128]{3,2,0,1:T(8,128)(2,1)} %fusion.74) | data formatting | bytes 33554432 | tf_op jit(solution)/shard_map/stack | solution.py:98
  212.9 1.0 fusion.72
  215.0 1.0 fusion.70
  216.0 1.0 fusion.69
  217.1 1.0 fusion.68
  218.1 1.0 fusion.67
  219.1 1.0 fusion.66
  220.2 1.0 fusion.65
  223.3 1.0 fusion.62
  228.3 1.0 fusion.57
  230.4 1.0 fusion.55
  231.4 1.0 fusion.54
  232.5 1.0 fusion.53
  237.6 1.0 fusion.48
  242.7 1.0 fusion.43
  243.7 1.0 fusion.42
  244.8 6.0 %all-gather.11.cloned.1.call-done = f32[512,1024]{1,0:T(8,128)} async-done(((f32[32,1024]{1,0:T(8,128)}), f32[512,1024]{1,0:T(8,128)}) %all-gather.11.cloned.1.call-update) | async-done | bytes 2097168 | tf_op jit(solution)/shard_map/all_gather | solution.py:86
  250.7 3.2 copy.341
  253.9 54.6 %all-gather.9.cloned.1.call-done = bf16[64,32,1024]{2,1,0:T(8,128)(2,1)} async-done(((bf16[4,32,1024]{2,1,0:T(8,128)(2,1)}), bf16[64,32,1024]{2,1,0:T(8,128)(2,1)}) %all-gather.9.cloned.1.call-update) | async-done | bytes 4194320 | tf_op jit(solution)/shard_map/all_gather | solution.py:84
  308.4 2.6 fusion.172
  311.1 1.2 copy.356
  312.5 18.1 %fusion = f32[512,32]{1,0:T(8,128)} fusion(bf16[32,16384]{1,0:T(8,128)(2,1)S(1)} %bitcast.576, bf16[64,8,128,128]{3,2,1,0:T(8,128)(2,1)} %bitcast.218), kind=kOutput, calls=%fused_computation.4 | convolution fusion | flops 536870912 | bytes 17891328 | tf_op jit(solution)/shard_map/dot_general | solution.py:99
  330.6 24.1 %fusion.2 = f32[512,32]{1,0:T(8,128)} fusion(bf16[32,16384]{1,0:T(8,128)(2,1)} %bitcast.578, bf16[64,8,128,128]{3,2,1,0:T(8,128)(2,1)} %bitcast.218), kind=kOutput, calls=%fused_computation.6 | convolution fusion | flops 536870912 | bytes 17891328 | tf_op jit(solution)/shard_map/dot_general | solution.py:99
  354.7 18.4 %fusion.8 = f32[512,32]{1,0:T(8,128)S(1)} fusion(bf16[32,16384]{1,0:T(8,128)(2,1)} %bitcast.577, bf16[64,8,128,128]{3,2,1,0:T(8,128)(2,1)S(1)} %bitcast.546), kind=kOutput, calls=%fused_computation.12 | convolution fusion | flops 536870912 | bytes 17891328 | tf_op jit(solution)/shard_map/dot_general | solution.py:99
  373.1 18.8 %fusion.10 = f32[512,32]{1,0:T(8,128)S(1)} fusion(bf16[32,16384]{1,0:T(8,128)(2,1)} %bitcast.579, bf16[64,8,128,128]{3,2,1,0:T(8,128)(2,1)S(1)} %bitcast.547), kind=kOutput, calls=%fused_computation.14 | convolution fusion | flops 536870912 | bytes 17891328 | tf_op jit(solution)/shard_map/dot_general | solution.py:99
  391.9 1.1 copy.355
  392.9 23.9 %fusion.4 = f32[512,32]{1,0:T(8,128)} fusion(bf16[32,16384]{1,0:T(8,128)(2,1)} %bitcast.582, bf16[64,8,128,128]{3,2,1,0:T(8,128)(2,1)} %bitcast.218), kind=kOutput, calls=%fused_computation.8 | convolution fusion | flops 536870912 | bytes 17891328 | tf_op jit(solution)/shard_map/dot_general | solution.py:99
  416.9 18.2 %fusion.12 = f32[512,32]{1,0:T(8,128)} fusion(bf16[32,16384]{1,0:T(8,128)(2,1)S(1)} %bitcast.583, bf16[64,8,128,128]{3,2,1,0:T(8,128)(2,1)S(1)} %bitcast.548), kind=kOutput, calls=%fused_computation.16 | convolution fusion | flops 536870912 | bytes 17891328 | tf_op jit(solution)/shard_map/dot_general | solution.py:99
  435.2 17.6 %fusion.6 = f32[512,32]{1,0:T(8,128)} fusion(bf16[32,16384]{1,0:T(8,128)(2,1)S(1)} %bitcast.580, bf16[64,8,128,128]{3,2,1,0:T(8,128)(2,1)} %bitcast.218), kind=kOutput, calls=%fused_computation.10 | convolution fusion | flops 536870912 | bytes 17891328 | tf_op jit(solution)/shard_map/dot_general | solution.py:99
  452.8 17.9 %fusion.14 = f32[512,32]{1,0:T(8,128)} fusion(bf16[32,16384]{1,0:T(8,128)(2,1)S(1)} %bitcast.581, bf16[64,8,128,128]{3,2,1,0:T(8,128)(2,1)S(1)} %bitcast.549), kind=kOutput, calls=%fused_computation.18 | convolution fusion | flops 536870912 | bytes 17891328 | tf_op jit(solution)/shard_map/dot_general | solution.py:99
  470.7 1.1 concatenate.71
  471.7 1.1 concatenate.68
  472.8 1.1 concatenate.62
  473.9 1.1 concatenate.65
  475.0 1.1 concatenate.61
  476.1 1.1 concatenate.64
  (133 shorter events, 57.8 us)
Async XLA Ops:
  14.9 40.1 %all-to-all-start = ((bf16[128,2,384]{2,1,0:T(2,128)(2,1)}), bf16[128,2,384]{2,1,0:T(2,128)(2,1)S(1)}, u32[]{:S(2)}, u32[]{:S(2)}) async-start(bf16[128,2,384]{2,1,0:T(2,128)(2,1)} %reshape.479), calls=%async_computation | async-start | bytes 393216 | tf_op jit(solution)/shard_map/all_to_all | solution.py:69
  41.3 23.8 %copy-start.2 = (s32[4]{0:T(128)S(1)}, s32[4]{0:T(128)}, u32[]{:S(2)}) copy-start(s32[4]{0:T(128)} %param.15) | copy-start | bytes 52
  44.6 25.0 %copy-start.3 = (f32[32]{0:T(128)S(1)}, f32[32]{0:T(128)}, u32[]{:S(2)}) copy-start(f32[32]{0:T(128)} %param.10) | copy-start | bytes 388
  54.9 89.8 %all-to-all-start.1 = ((bf16[128,4,6,1024]{3,1,2,0:T(4,128)(2,1)}), bf16[128,4,6,1024]{3,1,2,0:T(4,128)(2,1)}, u32[]{:S(2)}, u32[]{:S(2)}) async-start(bf16[128,4,6,1024]{3,1,2,0:T(4,128)(2,1)} %copy.285), calls=%async_computation.1 | async-start | bytes 12582912 | tf_op jit(solution)/shard_map/all_to_all | solution.py:68
  65.1 129.7 %all-gather.7.cloned.1.call-start = ((), (), s32[]{:S(2)}) async-start(), calls=%async_computation.2 | async-start | bytes 2359296 | tf_op jit(solution)/shard_map/all_gather | solution.py:83
  157.0 93.7 %all-gather.11.cloned.1.call-start = ((), (), s32[]{:S(2)}) async-start(), calls=%async_computation.4 | async-start | bytes 2228224 | tf_op jit(solution)/shard_map/all_gather | solution.py:86
  173.8 134.6 %all-gather.9.cloned.1.call-start = ((), (), s32[]{:S(2)}) async-start(), calls=%async_computation.3 | async-start | bytes 4456448 | tf_op jit(solution)/shard_map/all_gather | solution.py:84
  311.1 1.3 copy-start
  312.5 42.2 %slice-start = ((s8[16777216]{0:T(1024)(128)(4,1)}), s8[4194304]{0:T(1024)(128)(4,1)S(1)}, s32[]{:S(2)}) async-start(s8[16777216]{0:T(1024)(128)(4,1)} %bitcast.544), calls=%async_computation.5 | async-start | bytes 8388608
  312.5 42.2 %slice-start.1 = ((s8[16777216]{0:T(1024)(128)(4,1)}), s8[4194304]{0:T(1024)(128)(4,1)S(1)}, s32[]{:S(2)}) async-start(s8[16777216]{0:T(1024)(128)(4,1)} %bitcast.544), calls=%async_computation.6 | async-start | bytes 8388608
  330.6 24.1 %slice-start.2 = ((s8[16777216]{0:T(1024)(128)(4,1)}), s8[4194304]{0:T(1024)(128)(4,1)S(1)}, s32[]{:S(2)}) async-start(s8[16777216]{0:T(1024)(128)(4,1)} %bitcast.544), calls=%async_computation.7 | async-start | bytes 8388608
  330.6 24.1 %slice-start.3 = ((s8[16777216]{0:T(1024)(128)(4,1)}), s8[4194304]{0:T(1024)(128)(4,1)S(1)}, s32[]{:S(2)}) async-start(s8[16777216]{0:T(1024)(128)(4,1)} %bitcast.544), calls=%async_computation.8 | async-start | bytes 8388608
  392.9 23.9 %copy-start.1 = (bf16[4,8,16,1024]{3,1,2,0:T(8,128)(2,1)S(1)}, bf16[4,8,16,1024]{3,1,2,0:T(8,128)(2,1)}, u32[]{:S(2)}) copy-start(bf16[4,8,16,1024]{3,1,2,0:T(8,128)(2,1)} %copy.355) | copy-start | bytes 3145732
Sparse Core Ops, SparseCore 0:
  157.1 37.6 all-gather.6
  197.8 52.8 all-gather.10
  253.7 54.6 all-gather.8
